TPU v7x, 32 devices: a whole 2x2x4 slice. The times are simulated.
32 devices in a mesh: ta: 4 (over z), xyz: 8 (over y, x, core).
Axes of the slice: x: 2, y: 2, z: 4, core: 2. Of those that a mesh axis runs over, the one named last changes fastest.
Arguments:
- right_side: float32 [32, 4, 8, 4, 2, 2, 128], P(None, 'ta', 'xyz'), may hold values from -6 to 6
- coarse_links: bfloat16 [4, 8, 4, 2, 2, 9, 64, 128], P('ta', 'xyz'), may hold values from -3 to 3
- null_vectors: bfloat16 [4, 8, 4, 2, 2, 48, 128], P('ta', 'xyz'), may hold values from -0.29882812 to 0.29882812
- coarse_inverse: bfloat16 [4, 384, 384], P('ta', 'xyz'), may hold values from -2 to 2
Outputs:
- solution: float32 [32, 4, 8, 4, 2, 2, 128], P(None, 'ta', 'xyz')
- residual: float32 [32, 4, 8, 4, 2, 2, 128], P(None, 'ta', 'xyz')
All inputs are finite; a program needn't handle non-finite values.
Results may differ from a plain program's by a relative error of at most 0.0075.
Values may be sent and summed in bfloat16 or wider, within the bound.
No kernel may reach another device: no remote copies, remote signals or barrier semaphores. Data moves between devices by JAX's collectives and lax.ppermute only.
A program may use at most 64 MiB of HBM per device.

v0:
```python
import jax
import jax.numpy as jnp
from jax import lax
from jax.sharding import PartitionSpec as P

OMEGA = 0.4
EPS = 1e-06


def from_behind(x, axis, by):
    length = lax.axis_size(axis)
    return lax.ppermute(x, axis, [(i, (i + by) % length) for i in range(length)])


def with_halo(cells, sides, width):
    for axis, dim in sides:
        count = lax.axis_size(axis)
        head = lax.slice_in_dim(cells, 0, width, axis=dim)
        tail = lax.slice_in_dim(cells, cells.shape[dim] - width, cells.shape[dim], axis=dim)
        cells = jnp.concatenate(
            [
                lax.ppermute(tail, axis, [(i, (i + 1) % count) for i in range(count)]),
                cells,
                lax.ppermute(head, axis, [((i + 1) % count, i) for i in range(count)]),
            ],
            axis=dim,
        )
    return cells


def fetch_face(face, stride, extent, toward):
    nearby = from_behind(face, "xyz", -toward * stride)
    across = from_behind(face, "xyz", toward * stride * (extent - 1))
    coord = lax.axis_index("xyz") // stride % extent
    boundary = extent - 1 if toward > 0 else 0
    return jnp.where(coord == boundary, across, nearby)


def both_sides(lowered, which, stride, extent):
    length = lowered.shape[which]
    from_upper = fetch_face(lax.slice_in_dim(lowered, 0, 1, axis=which), stride, extent, 1)
    from_lower = fetch_face(
        lax.slice_in_dim(lowered, length - 1, length, axis=which), stride, extent, -1
    )
    upper = jnp.concatenate([lax.slice_in_dim(lowered, 1, length, axis=which), from_upper], which)
    lower = jnp.concatenate(
        [from_lower, lax.slice_in_dim(lowered, 0, length - 1, axis=which)], which
    )
    return (upper, lower)


def apply_links(coarse_links, lowered):
    blocks_total = lax.axis_size("xyz")
    across_x = 2 + 2 * min(blocks_total // 64, 1)
    across_z = blocks_total // (across_x * across_x)
    upper_x, lower_x = both_sides(lowered, 5, 1, across_x)
    upper_y, lower_y = both_sides(lowered, 4, across_x, across_x)
    upper_z, lower_z = both_sides(lowered, 3, across_x * across_x, across_z)
    padded = with_halo(lowered, (("ta", 1),), 1)
    upper_t = padded[:, 2:]
    lower_t = padded[:, :-2]
    stacked = jnp.stack(
        [lowered, upper_x, lower_x, upper_y, lower_y, upper_z, lower_z, upper_t, lower_t], 2
    )
    half_width = lowered.shape[-1] // 2
    real_part = stacked[..., :half_width]
    imag_part = stacked[..., half_width:]
    real_input = jnp.concatenate([real_part, -imag_part], -1)
    imag_input = jnp.concatenate([imag_part, real_part], -1)
    inputs = jnp.stack([real_input, imag_input], 0)
    result = jnp.einsum(
        "tbzyxdik,pntdbzyxk->pntbzyxi", coarse_links, inputs, preferred_element_type=jnp.float32
    )
    return jnp.concatenate([result[0], result[1]], -1)


def precondition(vector_in, null_vectors, coarse_inverse):
    lowered = vector_in.astype(jnp.bfloat16)
    coarse = jnp.einsum(
        "tbzyxjk,ntbzyxk->nj", null_vectors, lowered, preferred_element_type=jnp.float32
    ).astype(jnp.bfloat16)
    inverse_rows = coarse_inverse[0]
    correction = lax.dot_general(
        lax.all_gather(coarse, "xyz", axis=1, tiled=True),
        inverse_rows,
        (((1,), (1,)), ((), ())),
        preferred_element_type=jnp.float32,
    ).astype(jnp.bfloat16)
    prolonged = jnp.einsum(
        "tbzyxjk,nj->ntbzyxk", null_vectors, correction, preferred_element_type=jnp.float32
    )
    return OMEGA * vector_in + prolonged


def inner_rows(left_vec, right_vec):
    return jnp.sum(left_vec * right_vec, axis=(1, 2, 3, 4, 5, 6))


def scaled(weights, vector_in):
    return weights[:, None, None, None, None, None, None] * vector_in


def pair_products(image, residual):
    return lax.psum((inner_rows(image, image), inner_rows(image, residual)), ("ta", "xyz"))


def shards(right_side, coarse_links, null_vectors, coarse_inverse):
    residual = right_side
    direction_a = precondition(residual, null_vectors, coarse_inverse)
    image_a = apply_links(coarse_links, direction_a.astype(jnp.bfloat16))
    norm_a, correlation_a = pair_products(image_a, residual)
    step_a = correlation_a / (norm_a + EPS)
    solution = scaled(step_a, direction_a)
    residual = residual - scaled(step_a, image_a)
    direction_b = precondition(residual, null_vectors, coarse_inverse)
    image_b = apply_links(coarse_links, direction_b.astype(jnp.bfloat16))
    projection_sum = lax.psum(inner_rows(image_a, image_b), ("ta", "xyz"))
    beta_coef = projection_sum / (norm_a + EPS)
    image_b = image_b - scaled(beta_coef, image_a)
    direction_b = direction_b - scaled(beta_coef, direction_a)
    norm_b, correlation_b = pair_products(image_b, residual)
    step_b = correlation_b / (norm_b + EPS)
    solution = solution + scaled(step_b, direction_b)
    residual = residual - scaled(step_b, image_b)
    return (solution, residual)


def solution(mesh):
    in_specs = (
        P(None, "ta", "xyz", None, None, None, None),
        P("ta", "xyz", None, None, None, None, None, None),
        P("ta", "xyz", None, None, None, None, None),
        P("ta", "xyz", None),
    )
    out_specs = (
        P(None, "ta", "xyz", None, None, None, None),
        P(None, "ta", "xyz", None, None, None, None),
    )
    return jax.shard_map(shards, mesh=mesh, in_specs=in_specs, out_specs=out_specs, check_vma=False)
```

profile of v0, /device:TPU:0, one launch (start us, length us, event | category | flops | bytes accessed | tf_op | source)
XLA Modules:
  0.0 213.9 jit_solution(7676962154770344067)
XLA Ops:
  0.6 1.2 convert_bitcast_fusion.1
  1.8 1.1 fusion.23
  2.9 10.7 %all-gather = bf16[8,48,32]{1,2,0:T(8,128)(2,1)S(1)} all-gather(bf16[1,48,32]{1,2,0:T(8,128)(2,1)S(1)} %fusion.23), channel_id=1, replica_groups=mesh['ta'=4,'xyz'=8] {'xyz'}, dimensions={0}, use_global_device_ids=true | all-gather | bytes 27648 | tf_op jit(solution)/shard_map/all_gather | solution.py:84
  14.4 2.1 bitcast_dynamic-update-slice_fusion.5
  16.5 1.5 fusion.54
  18.0 1.5 collective-permute-start.7
  19.5 1.4 collective-permute-start.6
  20.9 1.5 fusion.55
  23.0 1.0 collective-permute-start.3
  24.0 1.7 fusion.53
  25.7 1.4 fusion.52
  27.1 1.7 collective-permute-start.2
  28.8 1.0 collective-permute-start.5
  31.5 1.1 collective-permute-start.4
  32.6 3.6 %collective-permute-start.10 = (bf16[32,1,1,4,2,2,128]{6,0,5,4,3,2,1:T(8,128)(2,1)}, bf16[32,1,1,4,2,2,128]{6,0,5,4,3,2,1:T(8,128)(2,1)S(1)}, u32[]{:S(2)}, u32[]{:S(2)}) collective-permute-start(bf16[32,1,1,4,2,2,128]{6,0,5,4,3,2,1:T(8,128)(2,1)} %get-tuple-element.23), channel_id=1, source_target_pairs={{8,0},{16,8},{24,16},{0,24},{9,1},{17,9},{25,17},{1,25},{10,2},{18... | collective-permute-start | bytes 393224 | tf_op jit(solution)/shard_map/ppermute | solution.py:24
  37.1 1.5 collective-permute-start.9
  41.1 2.5 %collective-permute-done.8 = bf16[32,1,1,1,2,2,128]{6,0,5,4,3,2,1:T(8,128)(2,1)S(1)} collective-permute-done((bf16[32,1,1,1,2,2,128]{6,0,5,4,3,2,1:T(8,128)(2,1)S(1)}, bf16[32,1,1,1,2,2,128]{6,0,5,4,3,2,1:T(8,128)(2,1)S(1)}, u32[]{:S(2)}, u32[]{:S(2)}) %collective-permute-start.8) | collective-permute-done | bytes 32800 | tf_op jit(solution)/shard_map/ppermute | solution.py:12
  48.6 38.7 %all-reduce.1 = (f32[32]{0:T(128)S(1)}, f32[32]{0:T(128)S(1)}) all-reduce(f32[32]{0:T(128)S(1)} %get-tuple-element.11, f32[32]{0:T(128)S(1)} %get-tuple-element.10), channel_id=1, replica_groups=mesh['ta'=4,'xyz'=8] {'ta','xyz'}, use_global_device_ids=true, to_apply=%region_1.2 | all-reduce | flops 64 | bytes 512 | tf_op jit(solution)/shard_map/psum | solution.py:104
  88.3 10.0 %all-gather.1 = bf16[8,48,32]{1,2,0:T(8,128)(2,1)S(1)} all-gather(bf16[1,48,32]{1,2,0:T(8,128)(2,1)S(1)} %fusion.22), channel_id=1, replica_groups=mesh['ta'=4,'xyz'=8] {'xyz'}, dimensions={0}, use_global_device_ids=true | all-gather | bytes 27648 | tf_op jit(solution)/shard_map/all_gather | solution.py:84
  99.0 2.1 bitcast_dynamic-update-slice_fusion.2
  103.0 1.4 collective-permute-start.13
  106.8 2.4 %collective-permute-start.18 = (bf16[32,1,1,4,1,2,128]{6,0,5,4,3,2,1:T(8,128)(2,1)S(1)}, bf16[32,1,1,4,1,2,128]{6,0,5,4,3,2,1:T(8,128)(2,1)S(1)}, u32[]{:S(2)}, u32[]{:S(2)}) collective-permute-start(bf16[32,1,1,4,1,2,128]{6,0,5,4,3,2,1:T(8,128)(2,1)S(1)} %get-tuple-element.36), channel_id=1, source_target_pairs={{0,6},{1,7},{2,0},{3,1},{4,2},{5,3},{6,4},{7,5},{8,14},{9,15},{10,... | collective-permute-start | bytes 196616 | tf_op jit(solution)/shard_map/ppermute | solution.py:12
  109.2 2.6 %collective-permute-start.14 = (bf16[32,1,1,4,2,1,128]{6,0,5,4,3,2,1:T(8,128)(2,1)S(1)}, bf16[32,1,1,4,2,1,128]{6,0,5,4,3,2,1:T(8,128)(2,1)S(1)}, u32[]{:S(2)}, u32[]{:S(2)}) collective-permute-start(bf16[32,1,1,4,2,1,128]{6,0,5,4,3,2,1:T(8,128)(2,1)S(1)} %get-tuple-element.38), channel_id=1, source_target_pairs={{0,7},{1,0},{2,1},{3,2},{4,3},{5,4},{6,5},{7,6},{8,15},{9,8},{10,9... | collective-permute-start | bytes 196616 | tf_op jit(solution)/shard_map/ppermute | solution.py:12
  111.8 2.7 %collective-permute-done.15 = bf16[32,1,1,4,2,1,128]{6,0,5,4,3,2,1:T(8,128)(2,1)S(1)} collective-permute-done((bf16[32,1,1,4,2,1,128]{6,0,5,4,3,2,1:T(8,128)(2,1)S(1)}, bf16[32,1,1,4,2,1,128]{6,0,5,4,3,2,1:T(8,128)(2,1)S(1)}, u32[]{:S(2)}, u32[]{:S(2)}) %collective-permute-start.15) | collective-permute-done | bytes 65568 | tf_op jit(solution)/shard_map/ppermute | solution.py:12
  114.5 2.1 %collective-permute-start.22 = (bf16[32,1,1,4,2,2,128]{6,0,5,4,3,2,1:T(8,128)(2,1)S(1)}, bf16[32,1,1,4,2,2,128]{6,0,5,4,3,2,1:T(8,128)(2,1)S(1)}, u32[]{:S(2)}, u32[]{:S(2)}) collective-permute-start(bf16[32,1,1,4,2,2,128]{6,0,5,4,3,2,1:T(8,128)(2,1)S(1)} %copy-done.5), channel_id=1, source_target_pairs={{8,0},{16,8},{24,16},{0,24},{9,1},{17,9},{25,17},{1,25},{10,2},{18... | collective-permute-start | bytes 393224 | tf_op jit(solution)/shard_map/ppermute | solution.py:24
  116.7 2.0 collective-permute-start.23
  118.7 1.0 collective-permute-done.16
  119.7 1.2 collective-permute-start.21
  121.9 3.0 %collective-permute-done.20 = bf16[32,1,1,1,2,2,128]{6,0,5,4,3,2,1:T(8,128)(2,1)S(1)} collective-permute-done((bf16[32,1,1,1,2,2,128]{6,0,5,4,3,2,1:T(8,128)(2,1)S(1)}, bf16[32,1,1,1,2,2,128]{6,0,5,4,3,2,1:T(8,128)(2,1)S(1)}, u32[]{:S(2)}, u32[]{:S(2)}) %collective-permute-start.20) | collective-permute-done | bytes 32800 | tf_op jit(solution)/shard_map/ppermute | solution.py:12
  129.9 39.7 %psum.37 = f32[32]{0:T(128)S(1)} all-reduce(f32[32]{0:T(128)S(1)} %multiply_reduce_fusion.2), channel_id=1, replica_groups=mesh['ta'=4,'xyz'=8] {'ta','xyz'}, use_global_device_ids=true, to_apply=%region_5.6 | all-reduce | flops 32 | bytes 256 | tf_op jit(solution)/shard_map/psum | solution.py:117
  170.6 40.1 %all-reduce = (f32[32]{0:T(128)S(1)}, f32[32]{0:T(128)S(1)}) all-reduce(f32[32]{0:T(128)S(1)} %get-tuple-element.9, f32[32]{0:T(128)S(1)} %get-tuple-element.8), channel_id=1, replica_groups=mesh['ta'=4,'xyz'=8] {'ta','xyz'}, use_global_device_ids=true, to_apply=%region_7.8 | all-reduce | flops 64 | bytes 512 | tf_op jit(solution)/shard_map/psum | solution.py:104
  210.8 1.3 multiply_subtract_fusion
  (107 shorter events, 25.9 us)
Async XLA Ops:
  0.6 45.9 %copy-start = (bf16[1,1,4,2,2,9,64,128]{7,6,5,4,3,2,1,0:T(8,128)(2,1)S(1)}, bf16[1,1,4,2,2,9,64,128]{7,6,5,4,3,2,1,0:T(8,128)(2,1)}, u32[]{:S(2)}) copy-start(bf16[1,1,4,2,2,9,64,128]{7,6,5,4,3,2,1,0:T(8,128)(2,1)} %param.5) | copy-start | bytes 7077892
  18.0 21.6 %collective-permute-start.7 = (bf16[32,1,1,4,1,2,128]{6,0,5,4,3,2,1:T(8,128)(2,1)}, bf16[32,1,1,4,1,2,128]{6,0,5,4,3,2,1:T(8,128)(2,1)}, u32[]{:S(2)}, u32[]{:S(2)}) collective-permute-start(bf16[32,1,1,4,1,2,128]{6,0,5,4,3,2,1:T(8,128)(2,1)} %get-tuple-element.44), channel_id=1, source_target_pairs={{0,2},{1,3},{2,4},{3,5},{4,6},{5,7},{6,0},{7,1},{8,10},{9,11},{10,... | collective-permute-start | bytes 196616 | tf_op jit(solution)/shard_map/ppermute | solution.py:12
  19.5 20.7 %collective-permute-start.6 = (bf16[32,1,1,4,1,2,128]{6,0,5,4,3,2,1:T(8,128)(2,1)}, bf16[32,1,1,4,1,2,128]{6,0,5,4,3,2,1:T(8,128)(2,1)}, u32[]{:S(2)}, u32[]{:S(2)}) collective-permute-start(bf16[32,1,1,4,1,2,128]{6,0,5,4,3,2,1:T(8,128)(2,1)} %get-tuple-element.44), channel_id=1, source_target_pairs={{0,6},{1,7},{2,0},{3,1},{4,2},{5,3},{6,4},{7,5},{8,14},{9,15},{10,... | collective-permute-start | bytes 196616 | tf_op jit(solution)/shard_map/ppermute | solution.py:12
  22.5 4.6 %collective-permute-start.1 = (bf16[32,1,1,4,2,1,128]{6,0,5,4,3,2,1:T(8,128)(2,1)}, bf16[32,1,1,4,2,1,128]{6,0,5,4,3,2,1:T(8,128)(2,1)}, u32[]{:S(2)}, u32[]{:S(2)}) collective-permute-start(bf16[32,1,1,4,2,1,128]{6,0,5,4,3,2,1:T(8,128)(2,1)} %get-tuple-element.47), channel_id=1, source_target_pairs={{0,7},{1,0},{2,1},{3,2},{4,3},{5,4},{6,5},{7,6},{8,15},{9,8},{10,9... | collective-permute-start | bytes 196616 | tf_op jit(solution)/shard_map/ppermute | solution.py:12
  22.5 6.3 %collective-permute-start = (bf16[32,1,1,4,2,1,128]{6,0,5,4,3,2,1:T(8,128)(2,1)}, bf16[32,1,1,4,2,1,128]{6,0,5,4,3,2,1:T(8,128)(2,1)}, u32[]{:S(2)}, u32[]{:S(2)}) collective-permute-start(bf16[32,1,1,4,2,1,128]{6,0,5,4,3,2,1:T(8,128)(2,1)} %get-tuple-element.47), channel_id=1, source_target_pairs={{0,1},{1,2},{2,3},{3,4},{4,5},{5,6},{6,7},{7,0},{8,9},{9,10},{10,1... | collective-permute-start | bytes 196616 | tf_op jit(solution)/shard_map/ppermute | solution.py:12
  23.0 8.5 %collective-permute-start.3 = (bf16[32,1,1,4,2,1,128]{6,0,5,4,3,2,1:T(8,128)(2,1)}, bf16[32,1,1,4,2,1,128]{6,0,5,4,3,2,1:T(8,128)(2,1)}, u32[]{:S(2)}, u32[]{:S(2)}) collective-permute-start(bf16[32,1,1,4,2,1,128]{6,0,5,4,3,2,1:T(8,128)(2,1)} %get-tuple-element.46), channel_id=1, source_target_pairs={{0,1},{1,2},{2,3},{3,4},{4,5},{5,6},{6,7},{7,0},{8,9},{9,10},{10,1... | collective-permute-start | bytes 196616 | tf_op jit(solution)/shard_map/ppermute | solution.py:12
  27.0 14.0 %copy-start.9 = (bf16[32,1,1,4,1,2,128]{6,0,5,4,3,2,1:T(8,128)(2,1)S(1)}, bf16[32,1,1,4,1,2,128]{6,0,5,4,3,2,1:T(8,128)(2,1)}, u32[]{:S(2)}) copy-start(bf16[32,1,1,4,1,2,128]{6,0,5,4,3,2,1:T(8,128)(2,1)} %get-tuple-element.45) | copy-start | bytes 196612
  27.0 16.5 %copy-start.8 = (bf16[32,1,1,3,2,2,128]{6,0,5,4,3,2,1:T(8,128)(2,1)S(1)}, bf16[32,1,1,3,2,2,128]{6,0,5,4,3,2,1:T(8,128)(2,1)}, u32[]{:S(2)}) copy-start(bf16[32,1,1,3,2,2,128]{6,0,5,4,3,2,1:T(8,128)(2,1)} %get-tuple-element.43) | copy-start | bytes 294916
  27.0 16.6 %copy-start.7 = (bf16[32,1,1,3,2,2,128]{6,0,5,4,3,2,1:T(8,128)(2,1)S(1)}, bf16[32,1,1,3,2,2,128]{6,0,5,4,3,2,1:T(8,128)(2,1)}, u32[]{:S(2)}) copy-start(bf16[32,1,1,3,2,2,128]{6,0,5,4,3,2,1:T(8,128)(2,1)} %get-tuple-element.42) | copy-start | bytes 294916
  27.1 5.5 %collective-permute-start.2 = (bf16[32,1,1,4,2,1,128]{6,0,5,4,3,2,1:T(8,128)(2,1)}, bf16[32,1,1,4,2,1,128]{6,0,5,4,3,2,1:T(8,128)(2,1)S(1)}, u32[]{:S(2)}, u32[]{:S(2)}) collective-permute-start(bf16[32,1,1,4,2,1,128]{6,0,5,4,3,2,1:T(8,128)(2,1)} %get-tuple-element.46), channel_id=1, source_target_pairs={{0,7},{1,0},{2,1},{3,2},{4,3},{5,4},{6,5},{7,6},{8,15},{9,8},{10,9... | collective-permute-start | bytes 196616 | tf_op jit(solution)/shard_map/ppermute | solution.py:12
  28.8 8.3 %collective-permute-start.5 = (bf16[32,1,1,4,1,2,128]{6,0,5,4,3,2,1:T(8,128)(2,1)}, bf16[32,1,1,4,1,2,128]{6,0,5,4,3,2,1:T(8,128)(2,1)S(1)}, u32[]{:S(2)}, u32[]{:S(2)}) collective-permute-start(bf16[32,1,1,4,1,2,128]{6,0,5,4,3,2,1:T(8,128)(2,1)} %get-tuple-element.45), channel_id=1, source_target_pairs={{0,6},{1,7},{2,0},{3,1},{4,2},{5,3},{6,4},{7,5},{8,14},{9,15},{10,... | collective-permute-start | bytes 196616 | tf_op jit(solution)/shard_map/ppermute | solution.py:12
  31.5 5.6 %collective-permute-start.4 = (bf16[32,1,1,4,1,2,128]{6,0,5,4,3,2,1:T(8,128)(2,1)}, bf16[32,1,1,4,1,2,128]{6,0,5,4,3,2,1:T(8,128)(2,1)S(1)}, u32[]{:S(2)}, u32[]{:S(2)}) collective-permute-start(bf16[32,1,1,4,1,2,128]{6,0,5,4,3,2,1:T(8,128)(2,1)} %get-tuple-element.45), channel_id=1, source_target_pairs={{0,2},{1,3},{2,4},{3,5},{4,6},{5,7},{6,0},{7,1},{8,10},{9,11},{10,... | collective-permute-start | bytes 196616 | tf_op jit(solution)/shard_map/ppermute | solution.py:12
  32.6 11.1 %collective-permute-start.10 = (bf16[32,1,1,4,2,2,128]{6,0,5,4,3,2,1:T(8,128)(2,1)}, bf16[32,1,1,4,2,2,128]{6,0,5,4,3,2,1:T(8,128)(2,1)S(1)}, u32[]{:S(2)}, u32[]{:S(2)}) collective-permute-start(bf16[32,1,1,4,2,2,128]{6,0,5,4,3,2,1:T(8,128)(2,1)} %get-tuple-element.23), channel_id=1, source_target_pairs={{8,0},{16,8},{24,16},{0,24},{9,1},{17,9},{25,17},{1,25},{10,2},{18... | collective-permute-start | bytes 393224 | tf_op jit(solution)/shard_map/ppermute | solution.py:24
  37.1 7.1 %collective-permute-start.11 = (bf16[32,1,1,4,2,2,128]{6,0,5,4,3,2,1:T(8,128)(2,1)}, bf16[32,1,1,4,2,2,128]{6,0,5,4,3,2,1:T(8,128)(2,1)S(1)}, u32[]{:S(2)}, u32[]{:S(2)}) collective-permute-start(bf16[32,1,1,4,2,2,128]{6,0,5,4,3,2,1:T(8,128)(2,1)} %get-tuple-element.23), channel_id=1, source_target_pairs={{0,8},{8,16},{16,24},{24,0},{1,9},{9,17},{17,25},{25,1},{2,10},{10... | collective-permute-start | bytes 393224 | tf_op jit(solution)/shard_map/ppermute | solution.py:22
  37.1 6.5 %collective-permute-start.9 = (bf16[32,1,1,1,2,2,128]{6,0,5,4,3,2,1:T(8,128)(2,1)}, bf16[32,1,1,1,2,2,128]{6,0,5,4,3,2,1:T(8,128)(2,1)S(1)}, u32[]{:S(2)}, u32[]{:S(2)}) collective-permute-start(bf16[32,1,1,1,2,2,128]{6,0,5,4,3,2,1:T(8,128)(2,1)} %get-tuple-element.40), channel_id=1, source_target_pairs={{0,4},{1,5},{2,6},{3,7},{4,0},{5,1},{6,2},{7,3},{8,12},{9,13},{10,... | collective-permute-start | bytes 98312 | tf_op jit(solution)/shard_map/ppermute | solution.py:12
  39.6 4.0 %collective-permute-start.8 = (bf16[32,1,1,1,2,2,128]{6,0,5,4,3,2,1:T(8,128)(2,1)S(1)}, bf16[32,1,1,1,2,2,128]{6,0,5,4,3,2,1:T(8,128)(2,1)S(1)}, u32[]{:S(2)}, u32[]{:S(2)}) collective-permute-start(bf16[32,1,1,1,2,2,128]{6,0,5,4,3,2,1:T(8,128)(2,1)S(1)} %copy-done.10), channel_id=1, source_target_pairs={{0,4},{1,5},{2,6},{3,7},{4,0},{5,1},{6,2},{7,3},{8,12},{9,13},{10,... | collective-permute-start | bytes 98312 | tf_op jit(solution)/shard_map/ppermute | solution.py:12
  47.5 40.7 %copy-start.6 = (bf16[1,1,4,2,2,48,128]{6,5,4,3,2,1,0:T(8,128)(2,1)S(1)}, bf16[1,1,4,2,2,48,128]{6,5,4,3,2,1,0:T(8,128)(2,1)}, u32[]{:S(2)}) copy-start(bf16[1,1,4,2,2,48,128]{6,5,4,3,2,1,0:T(8,128)(2,1)} %param.6) | copy-start | bytes 589828
  48.6 50.4 %copy-start.3 = (f32[32,1,1,4,2,2,128]{6,0,5,4,3,2,1:T(8,128)}, f32[32,1,1,4,2,2,128]{6,0,5,4,3,2,1:T(8,128)S(1)}, u32[]{:S(2)}) copy-start(f32[32,1,1,4,2,2,128]{6,0,5,4,3,2,1:T(8,128)S(1)} %get-tuple-element.21) | copy-start | bytes 786436
  101.2 13.4 %copy-start.5 = (bf16[32,1,1,4,2,2,128]{6,0,5,4,3,2,1:T(8,128)(2,1)S(1)}, bf16[32,1,1,4,2,2,128]{6,0,5,4,3,2,1:T(8,128)(2,1)}, u32[]{:S(2)}) copy-start(bf16[32,1,1,4,2,2,128]{6,0,5,4,3,2,1:T(8,128)(2,1)} %get-tuple-element.18) | copy-start | bytes 393220
  103.0 6.3 %collective-permute-start.13 = (bf16[32,1,1,4,2,1,128]{6,0,5,4,3,2,1:T(8,128)(2,1)S(1)}, bf16[32,1,1,4,2,1,128]{6,0,5,4,3,2,1:T(8,128)(2,1)S(1)}, u32[]{:S(2)}, u32[]{:S(2)}) collective-permute-start(bf16[32,1,1,4,2,1,128]{6,0,5,4,3,2,1:T(8,128)(2,1)S(1)} %get-tuple-element.39), channel_id=1, source_target_pairs={{0,7},{1,0},{2,1},{3,2},{4,3},{5,4},{6,5},{7,6},{8,15},{9,8},{10,9... | collective-permute-start | bytes 196616 | tf_op jit(solution)/shard_map/ppermute | solution.py:12
  104.4 7.4 %collective-permute-start.12 = (bf16[32,1,1,4,2,1,128]{6,0,5,4,3,2,1:T(8,128)(2,1)S(1)}, bf16[32,1,1,4,2,1,128]{6,0,5,4,3,2,1:T(8,128)(2,1)S(1)}, u32[]{:S(2)}, u32[]{:S(2)}) collective-permute-start(bf16[32,1,1,4,2,1,128]{6,0,5,4,3,2,1:T(8,128)(2,1)S(1)} %get-tuple-element.39), channel_id=1, source_target_pairs={{0,1},{1,2},{2,3},{3,4},{4,5},{5,6},{6,7},{7,0},{8,9},{9,10},{10,1... | collective-permute-start | bytes 196616 | tf_op jit(solution)/shard_map/ppermute | solution.py:12
  106.2 14.8 %collective-permute-start.19 = (bf16[32,1,1,4,1,2,128]{6,0,5,4,3,2,1:T(8,128)(2,1)S(1)}, bf16[32,1,1,4,1,2,128]{6,0,5,4,3,2,1:T(8,128)(2,1)S(1)}, u32[]{:S(2)}, u32[]{:S(2)}) collective-permute-start(bf16[32,1,1,4,1,2,128]{6,0,5,4,3,2,1:T(8,128)(2,1)S(1)} %get-tuple-element.36), channel_id=1, source_target_pairs={{0,2},{1,3},{2,4},{3,5},{4,6},{5,7},{6,0},{7,1},{8,10},{9,11},{10,... | collective-permute-start | bytes 196616 | tf_op jit(solution)/shard_map/ppermute | solution.py:12
  106.8 15.1 %collective-permute-start.18 = (bf16[32,1,1,4,1,2,128]{6,0,5,4,3,2,1:T(8,128)(2,1)S(1)}, bf16[32,1,1,4,1,2,128]{6,0,5,4,3,2,1:T(8,128)(2,1)S(1)}, u32[]{:S(2)}, u32[]{:S(2)}) collective-permute-start(bf16[32,1,1,4,1,2,128]{6,0,5,4,3,2,1:T(8,128)(2,1)S(1)} %get-tuple-element.36), channel_id=1, source_target_pairs={{0,6},{1,7},{2,0},{3,1},{4,2},{5,3},{6,4},{7,5},{8,14},{9,15},{10,... | collective-permute-start | bytes 196616 | tf_op jit(solution)/shard_map/ppermute | solution.py:12
  109.2 5.4 %collective-permute-start.15 = (bf16[32,1,1,4,2,1,128]{6,0,5,4,3,2,1:T(8,128)(2,1)S(1)}, bf16[32,1,1,4,2,1,128]{6,0,5,4,3,2,1:T(8,128)(2,1)S(1)}, u32[]{:S(2)}, u32[]{:S(2)}) collective-permute-start(bf16[32,1,1,4,2,1,128]{6,0,5,4,3,2,1:T(8,128)(2,1)S(1)} %get-tuple-element.38), channel_id=1, source_target_pairs={{0,1},{1,2},{2,3},{3,4},{4,5},{5,6},{6,7},{7,0},{8,9},{9,10},{10,1... | collective-permute-start | bytes 196616 | tf_op jit(solution)/shard_map/ppermute | solution.py:12
  109.2 5.3 %collective-permute-start.14 = (bf16[32,1,1,4,2,1,128]{6,0,5,4,3,2,1:T(8,128)(2,1)S(1)}, bf16[32,1,1,4,2,1,128]{6,0,5,4,3,2,1:T(8,128)(2,1)S(1)}, u32[]{:S(2)}, u32[]{:S(2)}) collective-permute-start(bf16[32,1,1,4,2,1,128]{6,0,5,4,3,2,1:T(8,128)(2,1)S(1)} %get-tuple-element.38), channel_id=1, source_target_pairs={{0,7},{1,0},{2,1},{3,2},{4,3},{5,4},{6,5},{7,6},{8,15},{9,8},{10,9... | collective-permute-start | bytes 196616 | tf_op jit(solution)/shard_map/ppermute | solution.py:12
  111.8 4.9 %collective-permute-start.17 = (bf16[32,1,1,4,1,2,128]{6,0,5,4,3,2,1:T(8,128)(2,1)S(1)}, bf16[32,1,1,4,1,2,128]{6,0,5,4,3,2,1:T(8,128)(2,1)S(1)}, u32[]{:S(2)}, u32[]{:S(2)}) collective-permute-start(bf16[32,1,1,4,1,2,128]{6,0,5,4,3,2,1:T(8,128)(2,1)S(1)} %get-tuple-element.37), channel_id=1, source_target_pairs={{0,6},{1,7},{2,0},{3,1},{4,2},{5,3},{6,4},{7,5},{8,14},{9,15},{10,... | collective-permute-start | bytes 196616 | tf_op jit(solution)/shard_map/ppermute | solution.py:12
  114.5 5.2 %collective-permute-start.16 = (bf16[32,1,1,4,1,2,128]{6,0,5,4,3,2,1:T(8,128)(2,1)S(1)}, bf16[32,1,1,4,1,2,128]{6,0,5,4,3,2,1:T(8,128)(2,1)S(1)}, u32[]{:S(2)}, u32[]{:S(2)}) collective-permute-start(bf16[32,1,1,4,1,2,128]{6,0,5,4,3,2,1:T(8,128)(2,1)S(1)} %get-tuple-element.37), channel_id=1, source_target_pairs={{0,2},{1,3},{2,4},{3,5},{4,6},{5,7},{6,0},{7,1},{8,10},{9,11},{10,... | collective-permute-start | bytes 196616 | tf_op jit(solution)/shard_map/ppermute | solution.py:12
  114.5 10.5 %collective-permute-start.22 = (bf16[32,1,1,4,2,2,128]{6,0,5,4,3,2,1:T(8,128)(2,1)S(1)}, bf16[32,1,1,4,2,2,128]{6,0,5,4,3,2,1:T(8,128)(2,1)S(1)}, u32[]{:S(2)}, u32[]{:S(2)}) collective-permute-start(bf16[32,1,1,4,2,2,128]{6,0,5,4,3,2,1:T(8,128)(2,1)S(1)} %copy-done.5), channel_id=1, source_target_pairs={{8,0},{16,8},{24,16},{0,24},{9,1},{17,9},{25,17},{1,25},{10,2},{18... | collective-permute-start | bytes 393224 | tf_op jit(solution)/shard_map/ppermute | solution.py:24
  116.7 8.3 %collective-permute-start.23 = (bf16[32,1,1,4,2,2,128]{6,0,5,4,3,2,1:T(8,128)(2,1)S(1)}, bf16[32,1,1,4,2,2,128]{6,0,5,4,3,2,1:T(8,128)(2,1)S(1)}, u32[]{:S(2)}, u32[]{:S(2)}) collective-permute-start(bf16[32,1,1,4,2,2,128]{6,0,5,4,3,2,1:T(8,128)(2,1)S(1)} %copy-done.5), channel_id=1, source_target_pairs={{0,8},{8,16},{16,24},{24,0},{1,9},{9,17},{17,25},{25,1},{2,10},{10... | collective-permute-start | bytes 393224 | tf_op jit(solution)/shard_map/ppermute | solution.py:22
  119.7 5.3 %collective-permute-start.21 = (bf16[32,1,1,1,2,2,128]{6,0,5,4,3,2,1:T(8,128)(2,1)S(1)}, bf16[32,1,1,1,2,2,128]{6,0,5,4,3,2,1:T(8,128)(2,1)S(1)}, u32[]{:S(2)}, u32[]{:S(2)}) collective-permute-start(bf16[32,1,1,1,2,2,128]{6,0,5,4,3,2,1:T(8,128)(2,1)S(1)} %get-tuple-element.32), channel_id=1, source_target_pairs={{0,4},{1,5},{2,6},{3,7},{4,0},{5,1},{6,2},{7,3},{8,12},{9,13},{10,... | collective-permute-start | bytes 98312 | tf_op jit(solution)/shard_map/ppermute | solution.py:12
  121.0 4.0 %collective-permute-start.20 = (bf16[32,1,1,1,2,2,128]{6,0,5,4,3,2,1:T(8,128)(2,1)S(1)}, bf16[32,1,1,1,2,2,128]{6,0,5,4,3,2,1:T(8,128)(2,1)S(1)}, u32[]{:S(2)}, u32[]{:S(2)}) collective-permute-start(bf16[32,1,1,1,2,2,128]{6,0,5,4,3,2,1:T(8,128)(2,1)S(1)} %get-tuple-element.33), channel_id=1, source_target_pairs={{0,4},{1,5},{2,6},{3,7},{4,0},{5,1},{6,2},{7,3},{8,12},{9,13},{10,... | collective-permute-start | bytes 98312 | tf_op jit(solution)/shard_map/ppermute | solution.py:12
  128.8 40.9 %copy-start.2 = (f32[32,1,1,4,2,2,128]{6,0,5,4,3,2,1:T(8,128)S(1)}, f32[32,1,1,4,2,2,128]{6,0,5,4,3,2,1:T(8,128)}, u32[]{:S(2)}) copy-start(f32[32,1,1,4,2,2,128]{6,0,5,4,3,2,1:T(8,128)} %get-tuple-element.20) | copy-start | bytes 786436
  (3 other events, 14.5 us)
where the time goes:
time: 215 us; the launch traced here: 214 us
  blocking collectives  139 us (65%)
  starting transfers between devices  27.3 us (13%)
  local copies, waits for them, and re-layouts  16.4 us (8%)
  other arithmetic  12.9 us (6%)
  waiting for transfers between devices  9.75 us (5%)
  matrix products  7.22 us (3%)
    psum x2, blocking collectives, pair_products(): lax.psum((inner_rows(image, image), inner_rows(image, residual)), ('ta',...  78.8 us
    psum x1, blocking collectives, shards(): projection_sum = lax.psum(inner_rows(image_a, image_b), ('ta', 'xyz'))  39.7 us
    all_gather x2, blocking collectives, precondition(): lax.all_gather(coarse, 'xyz', axis=1, tiled=True)  20.7 us
    ppermute x20, starting transfers between devices, from_behind(): lax.ppermute(x, axis, [(i, (i + by) % length) for i in range(length)])  19.5 us
    ppermute x20, waiting for transfers between devices, from_behind(): lax.ppermute(x, axis, [(i, (i + by) % length) for i in range(length)])  9.27 us
    ppermute x2, starting transfers between devices, with_halo(): lax.ppermute(head, axis, [((i + 1) % count, i) for i in range(count)])  5.75 us
    unnamed x28, local copies, waits for them, and re-layouts  5.09 us
    slice x4, local copies, waits for them, and re-layouts, both_sides(): lax.slice_in_dim(lowered, 1, length, axis=which)  4.87 us
  transfers between devices with their start and end apart: 24, of which 5 were waited for; matrix products, arithmetic and copies ran while one was open for 5% of the time, Pallas kernels for 0%

commit v1 on v0

--- a/solution.py
+++ b/solution.py
@@ -114,7 +114,7 @@
     residual = residual - scaled(step_a, image_a)
     direction_b = precondition(residual, null_vectors, coarse_inverse)
     image_b = apply_links(coarse_links, direction_b.astype(jnp.bfloat16))
-    projection_sum = lax.psum(inner_rows(image_a, image_b), ("ta", "xyz"))
+    projection_sum = lax.psum(lax.psum(inner_rows(image_a, image_b), "xyz"), "ta")
     beta_coef = projection_sum / (norm_a + EPS)
     image_b = image_b - scaled(beta_coef, image_a)
     direction_b = direction_b - scaled(beta_coef, direction_a)

time: 215 us -> 196 us (0.912)
  blocking collectives: 139 us -> 120 us
    psum x1 -> x2, blocking collectives: 39.7 us -> 23.2 us  [the longest x1 12.8 us: shards(): lax.psum(inner_rows(image_a, image_b), 'xyz')]
    psum x2, blocking collectives: 78.8 us -> 76.2 us  [pair_products(): lax.psum((inner_rows(image, image), inner_rows(image, residual)), ('ta',...]
  transfers between devices with their start and end apart: 24 -> 24, of which waited for: 5 -> 5; matrix products, arithmetic and copies ran while one was open for 5% -> 6% of each run, Pallas kernels for 0% -> 0%
where the time goes in v1:
time: 196 us; the launch traced here: 195 us
  blocking collectives  120 us (61%)
  starting transfers between devices  27.3 us (14%)
  local copies, waits for them, and re-layouts  16.4 us (8%)
  other arithmetic  12.9 us (7%)
  waiting for transfers between devices  9.75 us (5%)
  matrix products  7.22 us (4%)
    psum x2, blocking collectives, pair_products(): lax.psum((inner_rows(image, image), inner_rows(image, residual)), ('ta',...  76.2 us
    all_gather x2, blocking collectives, precondition(): lax.all_gather(coarse, 'xyz', axis=1, tiled=True)  20.7 us
    ppermute x20, starting transfers between devices, from_behind(): lax.ppermute(x, axis, [(i, (i + by) % length) for i in range(length)])  19.5 us
    psum x1, blocking collectives, shards(): lax.psum(inner_rows(image_a, image_b), 'xyz')  12.8 us
    psum x1, blocking collectives, shards(): lax.psum(lax.psum(inner_rows(image_a, image_b), 'xyz'), 'ta')  10.5 us
    ppermute x20, waiting for transfers between devices, from_behind(): lax.ppermute(x, axis, [(i, (i + by) % length) for i in range(length)])  9.26 us
    ppermute x2, starting transfers between devices, with_halo(): lax.ppermute(head, axis, [((i + 1) % count, i) for i in range(count)])  5.78 us
    unnamed x28, local copies, waits for them, and re-layouts  5.1 us
  transfers between devices with their start and end apart: 24, of which 5 were waited for; matrix products, arithmetic and copies ran while one was open for 6% of the time, Pallas kernels for 0%

profile of v1, /device:TPU:0, one launch (start us, length us, event | category | flops | bytes accessed | tf_op | source)
XLA Modules:
  0.0 194.9 jit_solution(15306928956577903759)
XLA Ops:
  0.6 1.2 convert_bitcast_fusion.1
  1.8 1.1 fusion.23
  2.9 10.7 %all-gather = bf16[8,48,32]{1,2,0:T(8,128)(2,1)S(1)} all-gather(bf16[1,48,32]{1,2,0:T(8,128)(2,1)S(1)} %fusion.23), channel_id=1, replica_groups=mesh['ta'=4,'xyz'=8] {'xyz'}, dimensions={0}, use_global_device_ids=true | all-gather | bytes 27648 | tf_op jit(solution)/shard_map/all_gather | solution.py:84
  14.4 2.1 %bitcast_dynamic-update-slice_fusion.5 = (bf16[32,1,9,1,4,2,2,128]{7,0,6,5,4,3,2,1:T(8,128)(2,1)S(1)}, bf16[32,1,1,4,2,2,128]{6,0,5,4,3,2,1:T(8,128)(2,1)}, f32[32,1,1,4,2,2,128]{6,0,5,4,3,2,1:T(8,128)}) fusion(bf16[1,1,4,2,2,48,128]{6,5,4,3,2,1,0:T(8,128)(2,1)} %param.6, bf16[384,32]{0,1:T(8,128)(2,1)} %reshape.330, bf16[1,48,384]{2,1,0:T(8,128)(2,1)} %param.7, ...), kind=kOutput, calls=%fused_computation.76 | convolution fusion | flops 7669247 | bytes 1044480 | tf_op jit(solution)/shard_map/tbzyxjk,nj->ntbzyxk/dot_general | solution.py:89
  16.5 1.5 fusion.54
  18.0 1.5 collective-permute-start.7
  19.5 1.4 collective-permute-start.6
  21.0 1.5 fusion.55
  23.0 1.0 collective-permute-start.3
  24.0 1.7 fusion.53
  25.7 1.4 fusion.52
  27.1 1.7 collective-permute-start.2
  31.5 1.1 collective-permute-start.4
  32.6 3.6 %collective-permute-start.10 = (bf16[32,1,1,4,2,2,128]{6,0,5,4,3,2,1:T(8,128)(2,1)}, bf16[32,1,1,4,2,2,128]{6,0,5,4,3,2,1:T(8,128)(2,1)S(1)}, u32[]{:S(2)}, u32[]{:S(2)}) collective-permute-start(bf16[32,1,1,4,2,2,128]{6,0,5,4,3,2,1:T(8,128)(2,1)} %get-tuple-element.23), channel_id=1, source_target_pairs={{8,0},{16,8},{24,16},{0,24},{9,1},{17,9},{25,17},{1,25},{10,2},{18... | collective-permute-start | bytes 393224 | tf_op jit(solution)/shard_map/ppermute | solution.py:24
  37.2 1.5 collective-permute-start.9
  41.1 2.5 %collective-permute-done.8 = bf16[32,1,1,1,2,2,128]{6,0,5,4,3,2,1:T(8,128)(2,1)S(1)} collective-permute-done((bf16[32,1,1,1,2,2,128]{6,0,5,4,3,2,1:T(8,128)(2,1)S(1)}, bf16[32,1,1,1,2,2,128]{6,0,5,4,3,2,1:T(8,128)(2,1)S(1)}, u32[]{:S(2)}, u32[]{:S(2)}) %collective-permute-start.8) | collective-permute-done | bytes 32800 | tf_op jit(solution)/shard_map/ppermute | solution.py:12
  48.6 38.6 %all-reduce.1 = (f32[32]{0:T(128)S(1)}, f32[32]{0:T(128)S(1)}) all-reduce(f32[32]{0:T(128)S(1)} %get-tuple-element.11, f32[32]{0:T(128)S(1)} %get-tuple-element.10), channel_id=1, replica_groups=mesh['ta'=4,'xyz'=8] {'ta','xyz'}, use_global_device_ids=true, to_apply=%region_1.2 | all-reduce | flops 64 | bytes 512 | tf_op jit(solution)/shard_map/psum | solution.py:104
  88.3 10.0 %all-gather.1 = bf16[8,48,32]{1,2,0:T(8,128)(2,1)S(1)} all-gather(bf16[1,48,32]{1,2,0:T(8,128)(2,1)S(1)} %fusion.22), channel_id=1, replica_groups=mesh['ta'=4,'xyz'=8] {'xyz'}, dimensions={0}, use_global_device_ids=true | all-gather | bytes 27648 | tf_op jit(solution)/shard_map/all_gather | solution.py:84
  99.0 2.1 %bitcast_dynamic-update-slice_fusion.2 = (bf16[32,1,9,1,4,2,2,128]{7,0,6,5,4,3,2,1:T(8,128)(2,1)S(1)}, bf16[32,1,1,4,2,2,128]{6,0,5,4,3,2,1:T(8,128)(2,1)}, f32[32,1,1,4,2,2,128]{6,0,5,4,3,2,1:T(8,128)}) fusion(bf16[1,1,4,2,2,48,128]{6,5,4,3,2,1,0:T(8,128)(2,1)} %param.6, bf16[384,32]{0,1:T(8,128)(2,1)} %reshape.332, bf16[1,48,384]{2,1,0:T(8,128)(2,1)} %param.7, ...), kind=kOutput, calls=%fused_computation.73 | convolution fusion | flops 7669247 | bytes 1044480 | tf_op jit(solution)/shard_map/tbzyxjk,nj->ntbzyxk/dot_general | solution.py:89
  103.0 1.5 collective-permute-start.13
  106.8 2.4 %collective-permute-start.18 = (bf16[32,1,1,4,1,2,128]{6,0,5,4,3,2,1:T(8,128)(2,1)S(1)}, bf16[32,1,1,4,1,2,128]{6,0,5,4,3,2,1:T(8,128)(2,1)S(1)}, u32[]{:S(2)}, u32[]{:S(2)}) collective-permute-start(bf16[32,1,1,4,1,2,128]{6,0,5,4,3,2,1:T(8,128)(2,1)S(1)} %get-tuple-element.36), channel_id=1, source_target_pairs={{0,6},{1,7},{2,0},{3,1},{4,2},{5,3},{6,4},{7,5},{8,14},{9,15},{10,... | collective-permute-start | bytes 196616 | tf_op jit(solution)/shard_map/ppermute | solution.py:12
  109.3 2.6 %collective-permute-start.14 = (bf16[32,1,1,4,2,1,128]{6,0,5,4,3,2,1:T(8,128)(2,1)S(1)}, bf16[32,1,1,4,2,1,128]{6,0,5,4,3,2,1:T(8,128)(2,1)S(1)}, u32[]{:S(2)}, u32[]{:S(2)}) collective-permute-start(bf16[32,1,1,4,2,1,128]{6,0,5,4,3,2,1:T(8,128)(2,1)S(1)} %get-tuple-element.38), channel_id=1, source_target_pairs={{0,7},{1,0},{2,1},{3,2},{4,3},{5,4},{6,5},{7,6},{8,15},{9,8},{10,9... | collective-permute-start | bytes 196616 | tf_op jit(solution)/shard_map/ppermute | solution.py:12
  111.9 2.7 %collective-permute-done.15 = bf16[32,1,1,4,2,1,128]{6,0,5,4,3,2,1:T(8,128)(2,1)S(1)} collective-permute-done((bf16[32,1,1,4,2,1,128]{6,0,5,4,3,2,1:T(8,128)(2,1)S(1)}, bf16[32,1,1,4,2,1,128]{6,0,5,4,3,2,1:T(8,128)(2,1)S(1)}, u32[]{:S(2)}, u32[]{:S(2)}) %collective-permute-start.15) | collective-permute-done | bytes 65568 | tf_op jit(solution)/shard_map/ppermute | solution.py:12
  114.5 2.2 %collective-permute-start.22 = (bf16[32,1,1,4,2,2,128]{6,0,5,4,3,2,1:T(8,128)(2,1)S(1)}, bf16[32,1,1,4,2,2,128]{6,0,5,4,3,2,1:T(8,128)(2,1)S(1)}, u32[]{:S(2)}, u32[]{:S(2)}) collective-permute-start(bf16[32,1,1,4,2,2,128]{6,0,5,4,3,2,1:T(8,128)(2,1)S(1)} %copy-done.5), channel_id=1, source_target_pairs={{8,0},{16,8},{24,16},{0,24},{9,1},{17,9},{25,17},{1,25},{10,2},{18... | collective-permute-start | bytes 393224 | tf_op jit(solution)/shard_map/ppermute | solution.py:24
  116.8 2.0 %collective-permute-start.23 = (bf16[32,1,1,4,2,2,128]{6,0,5,4,3,2,1:T(8,128)(2,1)S(1)}, bf16[32,1,1,4,2,2,128]{6,0,5,4,3,2,1:T(8,128)(2,1)S(1)}, u32[]{:S(2)}, u32[]{:S(2)}) collective-permute-start(bf16[32,1,1,4,2,2,128]{6,0,5,4,3,2,1:T(8,128)(2,1)S(1)} %copy-done.5), channel_id=1, source_target_pairs={{0,8},{8,16},{16,24},{24,0},{1,9},{9,17},{17,25},{25,1},{2,10},{10... | collective-permute-start | bytes 393224 | tf_op jit(solution)/shard_map/ppermute | solution.py:22
  118.7 1.0 collective-permute-done.16
  119.7 1.2 collective-permute-start.21
  121.9 3.1 %collective-permute-done.20 = bf16[32,1,1,1,2,2,128]{6,0,5,4,3,2,1:T(8,128)(2,1)S(1)} collective-permute-done((bf16[32,1,1,1,2,2,128]{6,0,5,4,3,2,1:T(8,128)(2,1)S(1)}, bf16[32,1,1,1,2,2,128]{6,0,5,4,3,2,1:T(8,128)(2,1)S(1)}, u32[]{:S(2)}, u32[]{:S(2)}) %collective-permute-start.20) | collective-permute-done | bytes 32800 | tf_op jit(solution)/shard_map/ppermute | solution.py:12
  130.0 12.8 %psum.44 = f32[32]{0:T(128)S(1)} all-reduce(f32[32]{0:T(128)S(1)} %multiply_reduce_fusion.2), channel_id=1, replica_groups=mesh['ta'=4,'xyz'=8] {'xyz'}, use_global_device_ids=true, to_apply=%region_5.6 | all-reduce | flops 32 | bytes 256 | tf_op jit(solution)/shard_map/psum | solution.py:117
  142.8 10.5 %psum.45 = f32[32]{0:T(128)S(1)} all-reduce(f32[32]{0:T(128)S(1)} %psum.44), channel_id=1, replica_groups=mesh['ta'=4,'xyz'=8] {'ta'}, use_global_device_ids=true, to_apply=%region_6.7 | all-reduce | flops 32 | bytes 256 | tf_op jit(solution)/shard_map/psum | solution.py:117
  154.2 37.6 %all-reduce = (f32[32]{0:T(128)S(1)}, f32[32]{0:T(128)S(1)}) all-reduce(f32[32]{0:T(128)S(1)} %get-tuple-element.9, f32[32]{0:T(128)S(1)} %get-tuple-element.8), channel_id=1, replica_groups=mesh['ta'=4,'xyz'=8] {'ta','xyz'}, use_global_device_ids=true, to_apply=%region_8.9 | all-reduce | flops 64 | bytes 512 | tf_op jit(solution)/shard_map/psum | solution.py:104
  191.8 1.3 multiply_subtract_fusion
  (108 shorter events, 26.8 us)
Async XLA Ops:
  0.6 45.9 %copy-start = (bf16[1,1,4,2,2,9,64,128]{7,6,5,4,3,2,1,0:T(8,128)(2,1)S(1)}, bf16[1,1,4,2,2,9,64,128]{7,6,5,4,3,2,1,0:T(8,128)(2,1)}, u32[]{:S(2)}) copy-start(bf16[1,1,4,2,2,9,64,128]{7,6,5,4,3,2,1,0:T(8,128)(2,1)} %param.5) | copy-start | bytes 7077892
  18.0 21.6 %collective-permute-start.7 = (bf16[32,1,1,4,1,2,128]{6,0,5,4,3,2,1:T(8,128)(2,1)}, bf16[32,1,1,4,1,2,128]{6,0,5,4,3,2,1:T(8,128)(2,1)}, u32[]{:S(2)}, u32[]{:S(2)}) collective-permute-start(bf16[32,1,1,4,1,2,128]{6,0,5,4,3,2,1:T(8,128)(2,1)} %get-tuple-element.44), channel_id=1, source_target_pairs={{0,2},{1,3},{2,4},{3,5},{4,6},{5,7},{6,0},{7,1},{8,10},{9,11},{10,... | collective-permute-start | bytes 196616 | tf_op jit(solution)/shard_map/ppermute | solution.py:12
  19.5 20.7 %collective-permute-start.6 = (bf16[32,1,1,4,1,2,128]{6,0,5,4,3,2,1:T(8,128)(2,1)}, bf16[32,1,1,4,1,2,128]{6,0,5,4,3,2,1:T(8,128)(2,1)}, u32[]{:S(2)}, u32[]{:S(2)}) collective-permute-start(bf16[32,1,1,4,1,2,128]{6,0,5,4,3,2,1:T(8,128)(2,1)} %get-tuple-element.44), channel_id=1, source_target_pairs={{0,6},{1,7},{2,0},{3,1},{4,2},{5,3},{6,4},{7,5},{8,14},{9,15},{10,... | collective-permute-start | bytes 196616 | tf_op jit(solution)/shard_map/ppermute | solution.py:12
  22.5 4.6 %collective-permute-start.1 = (bf16[32,1,1,4,2,1,128]{6,0,5,4,3,2,1:T(8,128)(2,1)}, bf16[32,1,1,4,2,1,128]{6,0,5,4,3,2,1:T(8,128)(2,1)}, u32[]{:S(2)}, u32[]{:S(2)}) collective-permute-start(bf16[32,1,1,4,2,1,128]{6,0,5,4,3,2,1:T(8,128)(2,1)} %get-tuple-element.47), channel_id=1, source_target_pairs={{0,7},{1,0},{2,1},{3,2},{4,3},{5,4},{6,5},{7,6},{8,15},{9,8},{10,9... | collective-permute-start | bytes 196616 | tf_op jit(solution)/shard_map/ppermute | solution.py:12
  22.5 6.3 %collective-permute-start = (bf16[32,1,1,4,2,1,128]{6,0,5,4,3,2,1:T(8,128)(2,1)}, bf16[32,1,1,4,2,1,128]{6,0,5,4,3,2,1:T(8,128)(2,1)}, u32[]{:S(2)}, u32[]{:S(2)}) collective-permute-start(bf16[32,1,1,4,2,1,128]{6,0,5,4,3,2,1:T(8,128)(2,1)} %get-tuple-element.47), channel_id=1, source_target_pairs={{0,1},{1,2},{2,3},{3,4},{4,5},{5,6},{6,7},{7,0},{8,9},{9,10},{10,1... | collective-permute-start | bytes 196616 | tf_op jit(solution)/shard_map/ppermute | solution.py:12
  23.0 8.5 %collective-permute-start.3 = (bf16[32,1,1,4,2,1,128]{6,0,5,4,3,2,1:T(8,128)(2,1)}, bf16[32,1,1,4,2,1,128]{6,0,5,4,3,2,1:T(8,128)(2,1)}, u32[]{:S(2)}, u32[]{:S(2)}) collective-permute-start(bf16[32,1,1,4,2,1,128]{6,0,5,4,3,2,1:T(8,128)(2,1)} %get-tuple-element.46), channel_id=1, source_target_pairs={{0,1},{1,2},{2,3},{3,4},{4,5},{5,6},{6,7},{7,0},{8,9},{9,10},{10,1... | collective-permute-start | bytes 196616 | tf_op jit(solution)/shard_map/ppermute | solution.py:12
  27.1 14.0 %copy-start.9 = (bf16[32,1,1,4,1,2,128]{6,0,5,4,3,2,1:T(8,128)(2,1)S(1)}, bf16[32,1,1,4,1,2,128]{6,0,5,4,3,2,1:T(8,128)(2,1)}, u32[]{:S(2)}) copy-start(bf16[32,1,1,4,1,2,128]{6,0,5,4,3,2,1:T(8,128)(2,1)} %get-tuple-element.45) | copy-start | bytes 196612
  27.1 16.5 %copy-start.8 = (bf16[32,1,1,3,2,2,128]{6,0,5,4,3,2,1:T(8,128)(2,1)S(1)}, bf16[32,1,1,3,2,2,128]{6,0,5,4,3,2,1:T(8,128)(2,1)}, u32[]{:S(2)}) copy-start(bf16[32,1,1,3,2,2,128]{6,0,5,4,3,2,1:T(8,128)(2,1)} %get-tuple-element.43) | copy-start | bytes 294916
  27.1 16.6 %copy-start.7 = (bf16[32,1,1,3,2,2,128]{6,0,5,4,3,2,1:T(8,128)(2,1)S(1)}, bf16[32,1,1,3,2,2,128]{6,0,5,4,3,2,1:T(8,128)(2,1)}, u32[]{:S(2)}) copy-start(bf16[32,1,1,3,2,2,128]{6,0,5,4,3,2,1:T(8,128)(2,1)} %get-tuple-element.42) | copy-start | bytes 294916
  27.1 5.5 %collective-permute-start.2 = (bf16[32,1,1,4,2,1,128]{6,0,5,4,3,2,1:T(8,128)(2,1)}, bf16[32,1,1,4,2,1,128]{6,0,5,4,3,2,1:T(8,128)(2,1)S(1)}, u32[]{:S(2)}, u32[]{:S(2)}) collective-permute-start(bf16[32,1,1,4,2,1,128]{6,0,5,4,3,2,1:T(8,128)(2,1)} %get-tuple-element.46), channel_id=1, source_target_pairs={{0,7},{1,0},{2,1},{3,2},{4,3},{5,4},{6,5},{7,6},{8,15},{9,8},{10,9... | collective-permute-start | bytes 196616 | tf_op jit(solution)/shard_map/ppermute | solution.py:12
  28.8 8.3 %collective-permute-start.5 = (bf16[32,1,1,4,1,2,128]{6,0,5,4,3,2,1:T(8,128)(2,1)}, bf16[32,1,1,4,1,2,128]{6,0,5,4,3,2,1:T(8,128)(2,1)S(1)}, u32[]{:S(2)}, u32[]{:S(2)}) collective-permute-start(bf16[32,1,1,4,1,2,128]{6,0,5,4,3,2,1:T(8,128)(2,1)} %get-tuple-element.45), channel_id=1, source_target_pairs={{0,6},{1,7},{2,0},{3,1},{4,2},{5,3},{6,4},{7,5},{8,14},{9,15},{10,... | collective-permute-start | bytes 196616 | tf_op jit(solution)/shard_map/ppermute | solution.py:12
  31.5 5.7 %collective-permute-start.4 = (bf16[32,1,1,4,1,2,128]{6,0,5,4,3,2,1:T(8,128)(2,1)}, bf16[32,1,1,4,1,2,128]{6,0,5,4,3,2,1:T(8,128)(2,1)S(1)}, u32[]{:S(2)}, u32[]{:S(2)}) collective-permute-start(bf16[32,1,1,4,1,2,128]{6,0,5,4,3,2,1:T(8,128)(2,1)} %get-tuple-element.45), channel_id=1, source_target_pairs={{0,2},{1,3},{2,4},{3,5},{4,6},{5,7},{6,0},{7,1},{8,10},{9,11},{10,... | collective-permute-start | bytes 196616 | tf_op jit(solution)/shard_map/ppermute | solution.py:12
  32.6 11.1 %collective-permute-start.10 = (bf16[32,1,1,4,2,2,128]{6,0,5,4,3,2,1:T(8,128)(2,1)}, bf16[32,1,1,4,2,2,128]{6,0,5,4,3,2,1:T(8,128)(2,1)S(1)}, u32[]{:S(2)}, u32[]{:S(2)}) collective-permute-start(bf16[32,1,1,4,2,2,128]{6,0,5,4,3,2,1:T(8,128)(2,1)} %get-tuple-element.23), channel_id=1, source_target_pairs={{8,0},{16,8},{24,16},{0,24},{9,1},{17,9},{25,17},{1,25},{10,2},{18... | collective-permute-start | bytes 393224 | tf_op jit(solution)/shard_map/ppermute | solution.py:24
  37.1 7.1 %collective-permute-start.11 = (bf16[32,1,1,4,2,2,128]{6,0,5,4,3,2,1:T(8,128)(2,1)}, bf16[32,1,1,4,2,2,128]{6,0,5,4,3,2,1:T(8,128)(2,1)S(1)}, u32[]{:S(2)}, u32[]{:S(2)}) collective-permute-start(bf16[32,1,1,4,2,2,128]{6,0,5,4,3,2,1:T(8,128)(2,1)} %get-tuple-element.23), channel_id=1, source_target_pairs={{0,8},{8,16},{16,24},{24,0},{1,9},{9,17},{17,25},{25,1},{2,10},{10... | collective-permute-start | bytes 393224 | tf_op jit(solution)/shard_map/ppermute | solution.py:22
  37.2 6.5 %collective-permute-start.9 = (bf16[32,1,1,1,2,2,128]{6,0,5,4,3,2,1:T(8,128)(2,1)}, bf16[32,1,1,1,2,2,128]{6,0,5,4,3,2,1:T(8,128)(2,1)S(1)}, u32[]{:S(2)}, u32[]{:S(2)}) collective-permute-start(bf16[32,1,1,1,2,2,128]{6,0,5,4,3,2,1:T(8,128)(2,1)} %get-tuple-element.40), channel_id=1, source_target_pairs={{0,4},{1,5},{2,6},{3,7},{4,0},{5,1},{6,2},{7,3},{8,12},{9,13},{10,... | collective-permute-start | bytes 98312 | tf_op jit(solution)/shard_map/ppermute | solution.py:12
  39.6 4.0 %collective-permute-start.8 = (bf16[32,1,1,1,2,2,128]{6,0,5,4,3,2,1:T(8,128)(2,1)S(1)}, bf16[32,1,1,1,2,2,128]{6,0,5,4,3,2,1:T(8,128)(2,1)S(1)}, u32[]{:S(2)}, u32[]{:S(2)}) collective-permute-start(bf16[32,1,1,1,2,2,128]{6,0,5,4,3,2,1:T(8,128)(2,1)S(1)} %copy-done.10), channel_id=1, source_target_pairs={{0,4},{1,5},{2,6},{3,7},{4,0},{5,1},{6,2},{7,3},{8,12},{9,13},{10,... | collective-permute-start | bytes 98312 | tf_op jit(solution)/shard_map/ppermute | solution.py:12
  47.5 40.6 %copy-start.6 = (bf16[1,1,4,2,2,48,128]{6,5,4,3,2,1,0:T(8,128)(2,1)S(1)}, bf16[1,1,4,2,2,48,128]{6,5,4,3,2,1,0:T(8,128)(2,1)}, u32[]{:S(2)}) copy-start(bf16[1,1,4,2,2,48,128]{6,5,4,3,2,1,0:T(8,128)(2,1)} %param.6) | copy-start | bytes 589828
  48.6 50.4 %copy-start.3 = (f32[32,1,1,4,2,2,128]{6,0,5,4,3,2,1:T(8,128)}, f32[32,1,1,4,2,2,128]{6,0,5,4,3,2,1:T(8,128)S(1)}, u32[]{:S(2)}) copy-start(f32[32,1,1,4,2,2,128]{6,0,5,4,3,2,1:T(8,128)S(1)} %get-tuple-element.21) | copy-start | bytes 786436
  101.2 13.4 %copy-start.5 = (bf16[32,1,1,4,2,2,128]{6,0,5,4,3,2,1:T(8,128)(2,1)S(1)}, bf16[32,1,1,4,2,2,128]{6,0,5,4,3,2,1:T(8,128)(2,1)}, u32[]{:S(2)}) copy-start(bf16[32,1,1,4,2,2,128]{6,0,5,4,3,2,1:T(8,128)(2,1)} %get-tuple-element.18) | copy-start | bytes 393220
  103.0 6.3 %collective-permute-start.13 = (bf16[32,1,1,4,2,1,128]{6,0,5,4,3,2,1:T(8,128)(2,1)S(1)}, bf16[32,1,1,4,2,1,128]{6,0,5,4,3,2,1:T(8,128)(2,1)S(1)}, u32[]{:S(2)}, u32[]{:S(2)}) collective-permute-start(bf16[32,1,1,4,2,1,128]{6,0,5,4,3,2,1:T(8,128)(2,1)S(1)} %get-tuple-element.39), channel_id=1, source_target_pairs={{0,7},{1,0},{2,1},{3,2},{4,3},{5,4},{6,5},{7,6},{8,15},{9,8},{10,9... | collective-permute-start | bytes 196616 | tf_op jit(solution)/shard_map/ppermute | solution.py:12
  104.4 7.4 %collective-permute-start.12 = (bf16[32,1,1,4,2,1,128]{6,0,5,4,3,2,1:T(8,128)(2,1)S(1)}, bf16[32,1,1,4,2,1,128]{6,0,5,4,3,2,1:T(8,128)(2,1)S(1)}, u32[]{:S(2)}, u32[]{:S(2)}) collective-permute-start(bf16[32,1,1,4,2,1,128]{6,0,5,4,3,2,1:T(8,128)(2,1)S(1)} %get-tuple-element.39), channel_id=1, source_target_pairs={{0,1},{1,2},{2,3},{3,4},{4,5},{5,6},{6,7},{7,0},{8,9},{9,10},{10,1... | collective-permute-start | bytes 196616 | tf_op jit(solution)/shard_map/ppermute | solution.py:12
  106.2 14.8 %collective-permute-start.19 = (bf16[32,1,1,4,1,2,128]{6,0,5,4,3,2,1:T(8,128)(2,1)S(1)}, bf16[32,1,1,4,1,2,128]{6,0,5,4,3,2,1:T(8,128)(2,1)S(1)}, u32[]{:S(2)}, u32[]{:S(2)}) collective-permute-start(bf16[32,1,1,4,1,2,128]{6,0,5,4,3,2,1:T(8,128)(2,1)S(1)} %get-tuple-element.36), channel_id=1, source_target_pairs={{0,2},{1,3},{2,4},{3,5},{4,6},{5,7},{6,0},{7,1},{8,10},{9,11},{10,... | collective-permute-start | bytes 196616 | tf_op jit(solution)/shard_map/ppermute | solution.py:12
  106.8 15.1 %collective-permute-start.18 = (bf16[32,1,1,4,1,2,128]{6,0,5,4,3,2,1:T(8,128)(2,1)S(1)}, bf16[32,1,1,4,1,2,128]{6,0,5,4,3,2,1:T(8,128)(2,1)S(1)}, u32[]{:S(2)}, u32[]{:S(2)}) collective-permute-start(bf16[32,1,1,4,1,2,128]{6,0,5,4,3,2,1:T(8,128)(2,1)S(1)} %get-tuple-element.36), channel_id=1, source_target_pairs={{0,6},{1,7},{2,0},{3,1},{4,2},{5,3},{6,4},{7,5},{8,14},{9,15},{10,... | collective-permute-start | bytes 196616 | tf_op jit(solution)/shard_map/ppermute | solution.py:12
  109.2 5.4 %collective-permute-start.15 = (bf16[32,1,1,4,2,1,128]{6,0,5,4,3,2,1:T(8,128)(2,1)S(1)}, bf16[32,1,1,4,2,1,128]{6,0,5,4,3,2,1:T(8,128)(2,1)S(1)}, u32[]{:S(2)}, u32[]{:S(2)}) collective-permute-start(bf16[32,1,1,4,2,1,128]{6,0,5,4,3,2,1:T(8,128)(2,1)S(1)} %get-tuple-element.38), channel_id=1, source_target_pairs={{0,1},{1,2},{2,3},{3,4},{4,5},{5,6},{6,7},{7,0},{8,9},{9,10},{10,1... | collective-permute-start | bytes 196616 | tf_op jit(solution)/shard_map/ppermute | solution.py:12
  109.3 5.3 %collective-permute-start.14 = (bf16[32,1,1,4,2,1,128]{6,0,5,4,3,2,1:T(8,128)(2,1)S(1)}, bf16[32,1,1,4,2,1,128]{6,0,5,4,3,2,1:T(8,128)(2,1)S(1)}, u32[]{:S(2)}, u32[]{:S(2)}) collective-permute-start(bf16[32,1,1,4,2,1,128]{6,0,5,4,3,2,1:T(8,128)(2,1)S(1)} %get-tuple-element.38), channel_id=1, source_target_pairs={{0,7},{1,0},{2,1},{3,2},{4,3},{5,4},{6,5},{7,6},{8,15},{9,8},{10,9... | collective-permute-start | bytes 196616 | tf_op jit(solution)/shard_map/ppermute | solution.py:12
  111.8 5.0 %collective-permute-start.17 = (bf16[32,1,1,4,1,2,128]{6,0,5,4,3,2,1:T(8,128)(2,1)S(1)}, bf16[32,1,1,4,1,2,128]{6,0,5,4,3,2,1:T(8,128)(2,1)S(1)}, u32[]{:S(2)}, u32[]{:S(2)}) collective-permute-start(bf16[32,1,1,4,1,2,128]{6,0,5,4,3,2,1:T(8,128)(2,1)S(1)} %get-tuple-element.37), channel_id=1, source_target_pairs={{0,6},{1,7},{2,0},{3,1},{4,2},{5,3},{6,4},{7,5},{8,14},{9,15},{10,... | collective-permute-start | bytes 196616 | tf_op jit(solution)/shard_map/ppermute | solution.py:12
  114.5 5.2 %collective-permute-start.16 = (bf16[32,1,1,4,1,2,128]{6,0,5,4,3,2,1:T(8,128)(2,1)S(1)}, bf16[32,1,1,4,1,2,128]{6,0,5,4,3,2,1:T(8,128)(2,1)S(1)}, u32[]{:S(2)}, u32[]{:S(2)}) collective-permute-start(bf16[32,1,1,4,1,2,128]{6,0,5,4,3,2,1:T(8,128)(2,1)S(1)} %get-tuple-element.37), channel_id=1, source_target_pairs={{0,2},{1,3},{2,4},{3,5},{4,6},{5,7},{6,0},{7,1},{8,10},{9,11},{10,... | collective-permute-start | bytes 196616 | tf_op jit(solution)/shard_map/ppermute | solution.py:12
  114.5 10.5 %collective-permute-start.22 = (bf16[32,1,1,4,2,2,128]{6,0,5,4,3,2,1:T(8,128)(2,1)S(1)}, bf16[32,1,1,4,2,2,128]{6,0,5,4,3,2,1:T(8,128)(2,1)S(1)}, u32[]{:S(2)}, u32[]{:S(2)}) collective-permute-start(bf16[32,1,1,4,2,2,128]{6,0,5,4,3,2,1:T(8,128)(2,1)S(1)} %copy-done.5), channel_id=1, source_target_pairs={{8,0},{16,8},{24,16},{0,24},{9,1},{17,9},{25,17},{1,25},{10,2},{18... | collective-permute-start | bytes 393224 | tf_op jit(solution)/shard_map/ppermute | solution.py:24
  116.8 8.3 %collective-permute-start.23 = (bf16[32,1,1,4,2,2,128]{6,0,5,4,3,2,1:T(8,128)(2,1)S(1)}, bf16[32,1,1,4,2,2,128]{6,0,5,4,3,2,1:T(8,128)(2,1)S(1)}, u32[]{:S(2)}, u32[]{:S(2)}) collective-permute-start(bf16[32,1,1,4,2,2,128]{6,0,5,4,3,2,1:T(8,128)(2,1)S(1)} %copy-done.5), channel_id=1, source_target_pairs={{0,8},{8,16},{16,24},{24,0},{1,9},{9,17},{17,25},{25,1},{2,10},{10... | collective-permute-start | bytes 393224 | tf_op jit(solution)/shard_map/ppermute | solution.py:22
  119.7 5.3 %collective-permute-start.21 = (bf16[32,1,1,1,2,2,128]{6,0,5,4,3,2,1:T(8,128)(2,1)S(1)}, bf16[32,1,1,1,2,2,128]{6,0,5,4,3,2,1:T(8,128)(2,1)S(1)}, u32[]{:S(2)}, u32[]{:S(2)}) collective-permute-start(bf16[32,1,1,1,2,2,128]{6,0,5,4,3,2,1:T(8,128)(2,1)S(1)} %get-tuple-element.32), channel_id=1, source_target_pairs={{0,4},{1,5},{2,6},{3,7},{4,0},{5,1},{6,2},{7,3},{8,12},{9,13},{10,... | collective-permute-start | bytes 98312 | tf_op jit(solution)/shard_map/ppermute | solution.py:12
  121.0 4.0 %collective-permute-start.20 = (bf16[32,1,1,1,2,2,128]{6,0,5,4,3,2,1:T(8,128)(2,1)S(1)}, bf16[32,1,1,1,2,2,128]{6,0,5,4,3,2,1:T(8,128)(2,1)S(1)}, u32[]{:S(2)}, u32[]{:S(2)}) collective-permute-start(bf16[32,1,1,1,2,2,128]{6,0,5,4,3,2,1:T(8,128)(2,1)S(1)} %get-tuple-element.33), channel_id=1, source_target_pairs={{0,4},{1,5},{2,6},{3,7},{4,0},{5,1},{6,2},{7,3},{8,12},{9,13},{10,... | collective-permute-start | bytes 98312 | tf_op jit(solution)/shard_map/ppermute | solution.py:12
  128.8 24.4 %copy-start.2 = (f32[32,1,1,4,2,2,128]{6,0,5,4,3,2,1:T(8,128)S(1)}, f32[32,1,1,4,2,2,128]{6,0,5,4,3,2,1:T(8,128)}, u32[]{:S(2)}) copy-start(f32[32,1,1,4,2,2,128]{6,0,5,4,3,2,1:T(8,128)} %get-tuple-element.20) | copy-start | bytes 786436
  (3 other events, 14.5 us)
